TPU v7x, 32 devices: a whole 2x2x4 slice. The times are simulated.
32 devices in a mesh: grp: 2 (over y), tile: 4 (over z), freq: 4 (over x, core).
Axes of the slice: x: 2, y: 2, z: 4, core: 2. Of those that a mesh axis runs over, the one named last changes fastest.
Arguments:
- sources: bfloat16 [4, 4, 2048, 512], P('freq', 'grp', 'tile'), parts along dimension 1, may hold values from -6 to 6
- v_factors: bfloat16 [4, 4, 2, 4, 112, 512], P('freq', 'tile', None, 'grp'), parts along dimension 3, may hold values from -0.1875 to 0.1875
- u_factors: bfloat16 [4, 4, 4, 112, 1024], P('freq', None, 'grp', None, 'tile'), parts along dimension 2, may hold values from -0.1875 to 0.1875
- tile_ranks: int32 [4, 4, 4], P('freq', 'grp', 'tile'), parts along dimension 1, may hold values from 16 to 112, as said below
- window_bounds: int32 [4, 1024, 512], P('grp', ('tile', 'freq')), parts along dimension 0, may hold values from 0 to 31, as said below
Outputs:
- windowed_traces: float32 [1024, 64, 512], P(('tile', 'freq'), 'grp'), parts along dimension 1
There are 2 independent parts, one for each index of `grp`. A program takes and returns all parts, laid end to end along the dimension named above; each array names one. Nothing has to cross between parts.
Inputs may be any that keep to these rules, and one draw needn't show every extreme that they name: `tile_ranks`: each tile's rank for each frequency; rank slots at or beyond it carry no coefficients. window_bounds[1] - window_bounds[0] lies between 8 and 16 for every receiver and virtual source.
All inputs are finite; a program needn't handle non-finite values.
Results may differ from a plain program's by a relative error of at most 0.0041.
Values may be sent and summed in bfloat16 or wider, within the bound.
No kernel may reach another device: no remote copies, remote signals or barrier semaphores. Data moves between devices by JAX's collectives and lax.ppermute only.
A program may use at most 64 MiB of HBM per device.

v0:
```python
import math
import jax
import jax.numpy as jnp
from jax import lax
from jax.sharding import PartitionSpec as P

NT = 32
first_bin = 2


def inverse_tables(count_freq, count_time):
    freq_index = jnp.arange(count_freq, dtype=jnp.int32)[:, None] + first_bin
    time_index = jnp.arange(count_time, dtype=jnp.int32)[None, :]
    phase_step = freq_index * time_index % count_time
    angles = phase_step.astype(jnp.float32) * (2.0 * math.pi / count_time)
    return (jnp.cos(angles), jnp.sin(angles))


def column_products(v_local, x_local, rank_local):
    products = lax.dot_general(
        v_local, x_local, (((3,), (1,)), ((), ())), preferred_element_type=jnp.float32
    )
    coef_real = products[:, 0, :, 0] - products[:, 1, :, 1]
    coef_imag = products[:, 0, :, 1] + products[:, 1, :, 0]
    slot_index = jnp.arange(v_local.shape[2], dtype=jnp.int32)
    live_slots = slot_index[None, :, None] < rank_local[:, None, None]
    coef_real = jnp.where(live_slots, coef_real, jnp.float32(0.0)).astype(jnp.bfloat16)
    coef_imag = jnp.where(live_slots, coef_imag, jnp.float32(0.0)).astype(jnp.bfloat16)
    return (coef_real, coef_imag)


def row_products(u_part, coef_part):
    return lax.dot_general(
        u_part, coef_part, (((0, 2), (0, 2)), ((), ())), preferred_element_type=jnp.float32
    )


def finish_spectrum(products):
    real_part = products[0, :, 0] - products[1, :, 1]
    imag_part = products[0, :, 1] + products[1, :, 0]
    return jnp.stack([real_part, imag_part], axis=0).astype(jnp.bfloat16)


def per_device(sources, v_factors, u_factors, tile_ranks, window_bounds):
    v_local = v_factors[0, 0]
    u_local = u_factors[0]
    coef_real, coef_imag = column_products(v_local, sources[0], tile_ranks[0, :, 0])
    sending = jnp.repeat(jnp.stack([coef_real, coef_imag], axis=1), 2, axis=0)

    def apply_whole(received, u_local=u_local):
        return finish_spectrum(row_products(u_local, received))

    spectrum = apply_whole(lax.all_to_all(sending, "tile", split_axis=0, concat_axis=0, tiled=True))
    spectrum_list = [spectrum]
    spectra = jnp.stack(spectrum_list, axis=0)
    received = lax.all_to_all(spectra, "freq", split_axis=2, concat_axis=0, tiled=True)
    count_freq = received.shape[0]
    cosine_table, sine_table = inverse_tables(count_freq, NT)
    widened = received.astype(jnp.float32)
    traces = jnp.einsum(
        "frs,fn->rns", widened[:, 0], cosine_table, precision=lax.Precision.HIGHEST
    ) - jnp.einsum("frs,fn->rns", widened[:, 1], sine_table, precision=lax.Precision.HIGHEST)
    traces = traces * (1.0 / math.sqrt(count_freq))
    time_index = jnp.arange(traces.shape[1], dtype=jnp.int32)[None, :, None]
    inside = (time_index >= window_bounds[0][:, None, :]) & (
        time_index < window_bounds[1][:, None, :]
    )
    return jnp.where(inside, traces, jnp.float32(0.0))


def solution(mesh):
    return jax.shard_map(
        per_device,
        mesh=mesh,
        in_specs=(
            P("freq", "grp", "tile", None),
            P("freq", "tile", None, "grp", None, None),
            P("freq", None, "grp", None, "tile"),
            P("freq", "grp", "tile"),
            P("grp", ("tile", "freq"), None),
        ),
        out_specs=P(("tile", "freq"), "grp", None),
        check_vma=False,
    )
```

profile of v0, /device:TPU:0, one launch (start us, length us, event | category | flops | bytes accessed | tf_op | source)
XLA Modules:
  0.0 53.6 jit_solution(12524646599114764560)
XLA Ops:
  0.0 0.0 copy-start
  0.0 0.8 %iota_compare_fusion.2 = pred[2,112]{1,0:T(4,128)(4,1)S(1)} fusion(s32[2]{0:T(128)} %bitcast.104), kind=kLoop, calls=%fused_computation.47 | loop fusion | flops 224 | bytes 232 | tf_op jit(solution)/shard_map/lt | solution.py:26
  0.8 0.4 copy-done
  1.2 1.7 %fusion.1 = f32[2,2,112,2,512]{4,2,3,1,0:T(8,128)S(1)} fusion(bf16[1,2,512,512]{3,2,1,0:T(8,128)(2,1)S(1)} %copy-done, bf16[1,1,2,2,112,512]{5,4,3,2,1,0:T(8,128)(2,1)} %param.6), kind=kOutput, calls=%fused_computation.5 | convolution fusion | flops 469762048 | bytes 3342336 | tf_op jit(solution)/shard_map/dot_general | solution.py:20
  2.9 0.0 copy-start.2
  2.9 0.2 fusion.13
  3.2 0.1 broadcast_in_dim.29
  3.3 29.0 %all_to_all.23 = bf16[4,2,112,512]{3,2,1,0:T(8,128)(2,1)S(1)} all-to-all(bf16[4,2,112,512]{3,2,1,0:T(8,128)(2,1)S(1)} %bitcast.100), channel_id=1, replica_groups=mesh['grp'=2,'tile'=4,'freq'=4] {'tile'}, dimensions={0} | all-to-all | bytes 1835008 | tf_op jit(solution)/shard_map/all_to_all | solution.py:53
  32.3 0.0 copy-done.2
  32.3 0.0 copy-start.1
  32.3 0.7 %convolution_bitcast_fusion = f32[2,256,2,512]{1,3,0,2:T(8,128)S(1)} fusion(bf16[4,2,112,512]{3,2,1,0:T(8,128)(2,1)S(1)} %all_to_all.23, bf16[1,4,2,112,256]{4,3,2,1,0:T(8,128)(2,1)S(1)} %copy-done.2), kind=kOutput, calls=%fused_computation.4 | convolution fusion | flops 469762048 | bytes 3473408 | tf_op jit(solution)/shard_map/dot_general | solution.py:33
  33.0 0.1 fusion.18
  33.1 0.1 fusion.17
  33.2 0.1 pad_maximum_fusion
  33.2 1.2 %copy.26 = bf16[1,2,256,512]{3,1,0,2:T(2,128)(2,1)} copy(bf16[1,2,256,512]{2,3,1,0:T(8,128)(2,1)S(1)} %pad_maximum_fusion) | data formatting | bytes 1048576 | tf_op jit(solution)/shard_map/stack | solution.py:41
  34.4 3.5 %all-to-all-start.1 = ((bf16[1,2,256,512]{3,1,0,2:T(2,128)(2,1)}), bf16[1,2,256,512]{3,1,0,2:T(2,128)(2,1)S(1)}, u32[]{:S(2)}, u32[]{:S(2)}) async-start(bf16[1,2,256,512]{3,1,0,2:T(2,128)(2,1)} %copy.26), calls=%async_computation.1 | async-start | bytes 1048576 | tf_op jit(solution)/shard_map/all_to_all | solution.py:56
  37.9 0.0 copy-done.1
  37.9 8.8 %all-to-all-done.1 = bf16[1,2,256,512]{3,1,0,2:T(2,128)(2,1)S(1)} async-done(((bf16[1,2,256,512]{3,1,0,2:T(2,128)(2,1)}), bf16[1,2,256,512]{3,1,0,2:T(2,128)(2,1)S(1)}, u32[]{:S(2)}, u32[]{:S(2)}) %all-to-all-start.1) | async-done | bytes 524320 | tf_op jit(solution)/shard_map/all_to_all | solution.py:56
  46.7 0.4 copy.48
  47.1 2.0 %fusion.19 = f32[32,64,512]{2,0,1:T(8,128)S(1)} fusion(bf16[4,2,64,512]{3,0,2,1:T(4,128)(2,1)S(1)} %bitcast.101, s32[4]{0:T(128)S(1)} %iota_add_fusion), kind=kOutput, calls=%fused_computation.34 | convolution fusion | flops 50333440 | bytes 4456960 | tf_op jit(solution)/shard_map/frs,fn->rns/dot_general | solution.py:60
  49.1 4.5 %bitcast_select_fusion = f32[64,32,512]{2,1,0:T(8,128)} fusion(f32[32,64,512]{2,0,1:T(8,128)S(1)} %fusion.19, s32[64,512]{1,0:T(8,128)S(1)} %get-tuple-element.8, s32[64,512]{1,0:T(8,128)S(1)} %get-tuple-element.7, bf16[4,2,64,512]{3,0,2,1:T(4,128)(2,1)S(1)} %bitcast.102, s32[4]{0:T(128)S(1)} %iota_add_fusion), kind=kOutput, calls=%fused_computation | convolution fusion | flops 56624896 | bytes 8913408 | tf_op jit(solution)/shard_map/frs,fn->rns/dot_general | solution.py:62
  (4 shorter events, 0.1 us)
Async XLA Ops:
  0.0 1.2 %copy-start = (bf16[1,2,512,512]{3,2,1,0:T(8,128)(2,1)S(1)}, bf16[1,2,512,512]{3,2,1,0:T(8,128)(2,1)}, u32[]{:S(2)}) copy-start(bf16[1,2,512,512]{3,2,1,0:T(8,128)(2,1)} %param.5) | copy-start | bytes 3145732
  2.9 29.4 %copy-start.2 = (bf16[1,4,2,112,256]{4,3,2,1,0:T(8,128)(2,1)S(1)}, bf16[1,4,2,112,256]{4,3,2,1,0:T(8,128)(2,1)}, u32[]{:S(2)}) copy-start(bf16[1,4,2,112,256]{4,3,2,1,0:T(8,128)(2,1)} %param.7) | copy-start | bytes 1376260
  32.3 5.6 %copy-start.1 = (s32[2,64,512]{2,1,0:T(8,128)S(1)}, s32[2,64,512]{2,1,0:T(8,128)}, u32[]{:S(2)}) copy-start(s32[2,64,512]{2,1,0:T(8,128)} %param.9) | copy-start | bytes 786436
  34.4 12.3 %all-to-all-start.1 = ((bf16[1,2,256,512]{3,1,0,2:T(2,128)(2,1)}), bf16[1,2,256,512]{3,1,0,2:T(2,128)(2,1)S(1)}, u32[]{:S(2)}, u32[]{:S(2)}) async-start(bf16[1,2,256,512]{3,1,0,2:T(2,128)(2,1)} %copy.26), calls=%async_computation.1 | async-start | bytes 1048576 | tf_op jit(solution)/shard_map/all_to_all | solution.py:56
where the time goes:
time: 53.9 us; the launch traced here: 53.6 us
  blocking collectives  29 us (54%)
  matrix products  8.92 us (17%)
  waiting for transfers between devices  8.76 us (16%)
  starting transfers between devices  3.47 us (6%)
  local copies, waits for them, and re-layouts  2.15 us (4%)
  other arithmetic  1.19 us (2%)
    all_to_all x1, blocking collectives, per_device(): lax.all_to_all(sending, 'tile', split_axis=0, concat_axis=0, tiled=True)  29 us
    all_to_all x1, waiting for transfers between devices, per_device(): lax.all_to_all(spectra, 'freq', split_axis=2, concat_axis=0, tiled=True)  8.76 us
    dot_general x1, matrix products, per_device(): jnp.einsum('frs,fn->rns', widened[:, 1], sine_table, precision=lax.Precis...  4.53 us
    all_to_all x1, starting transfers between devices, per_device(): lax.all_to_all(spectra, 'freq', split_axis=2, concat_axis=0, tiled=True)  3.47 us
    dot_general x1, matrix products, per_device(): jnp.einsum('frs,fn->rns', widened[:, 0], cosine_table, precision=lax.Prec...  2.01 us
    dot_general x1, matrix products, column_products(): lax.dot_general(v_local, x_local, (((3,), (1,)), ((), ())), preferred_ele...  1.65 us
    another operation x1, local copies, waits for them, and re-layouts, finish_spectrum(): return jnp.stack([real_part, imag_part], axis=0).astype(jnp.bfloat16)  1.18 us
  transfers between devices with their start and end apart: 1, of which 1 were waited for; matrix products, arithmetic and copies ran while one was open for 0% of the time, Pallas kernels for 0%

commit v1 on v0

--- a/solution.py
+++ b/solution.py
@@ -6,6 +6,30 @@
 
 NT = 32
 first_bin = 2
+
+
+def cut_along(x, dim, devices):
+    shape = x.shape
+    parts = x.reshape(*shape[:dim], devices, shape[dim] // devices, *shape[dim + 1 :])
+    return jnp.moveaxis(parts, dim, 0)
+
+
+def in_order(parts, dim):
+    shape = list(parts.shape[1:])
+    shape[dim] *= parts.shape[0]
+    return jnp.moveaxis(parts, 0, dim).reshape(shape)
+
+
+def sent_to_each(x, axis, split_dim, concat_dim):
+    size, position = (lax.axis_size(axis), lax.axis_index(axis))
+    parts = cut_along(x, split_dim, size)
+    out = parts
+    for step in range(1, size):
+        target, source = ((position + step) % size, (position - step) % size)
+        sent = lax.dynamic_index_in_dim(parts, target, 0)
+        other = lax.ppermute(sent, axis, [(i, (i + step) % size) for i in range(size)])
+        out = lax.dynamic_update_slice_in_dim(out, other, source, axis=0)
+    return in_order(out, concat_dim)
 
 
 def inverse_tables(count_freq, count_time):
@@ -50,7 +74,7 @@
     def apply_whole(received, u_local=u_local):
         return finish_spectrum(row_products(u_local, received))
 
-    spectrum = apply_whole(lax.all_to_all(sending, "tile", split_axis=0, concat_axis=0, tiled=True))
+    spectrum = apply_whole(sent_to_each(sending, "tile", 0, 0))
     spectrum_list = [spectrum]
     spectra = jnp.stack(spectrum_list, axis=0)
     received = lax.all_to_all(spectra, "freq", split_axis=2, concat_axis=0, tiled=True)

time: 53.9 us -> 50.5 us (0.937)
  blocking collectives: 29 us -> 0 us
  waiting for transfers between devices: 8.76 us -> 28 us
  starting transfers between devices: 3.47 us -> 9.59 us
    all_to_all x1 -> x0, blocking collectives: 29 us -> none  [per_device(): lax.all_to_all(sending, 'tile', split_axis=0, concat_axis=0, tiled=True)]
    ppermute x0 -> x3, waiting for transfers between devices: none -> 19.2 us  [sent_to_each(): lax.ppermute(sent, axis, [(i, (i + step) % size) for i in range(size)])]
    ppermute x0 -> x3, starting transfers between devices: none -> 6.11 us  [sent_to_each(): lax.ppermute(sent, axis, [(i, (i + step) % size) for i in range(size)])]
  transfers between devices with their start and end apart: 1 -> 4, of which waited for: 1 -> 3; matrix products, arithmetic and copies ran while one was open for 0% -> 0% of each run, Pallas kernels for 0% -> 0%
where the time goes in v1:
time: 50.5 us; the launch traced here: 50.2 us
  waiting for transfers between devices  28 us (55%)
  starting transfers between devices  9.59 us (19%)
  matrix products  8.92 us (18%)
  local copies, waits for them, and re-layouts  2.35 us (5%)
  other arithmetic  1.19 us (2%)
    ppermute x3, waiting for transfers between devices, sent_to_each(): lax.ppermute(sent, axis, [(i, (i + step) % size) for i in range(size)])  19.2 us
    all_to_all x1, waiting for transfers between devices, per_device(): lax.all_to_all(spectra, 'freq', split_axis=2, concat_axis=0, tiled=True)  8.76 us
    ppermute x3, starting transfers between devices, sent_to_each(): lax.ppermute(sent, axis, [(i, (i + step) % size) for i in range(size)])  6.11 us
    dot_general x1, matrix products, per_device(): jnp.einsum('frs,fn->rns', widened[:, 1], sine_table, precision=lax.Precis...  4.53 us
    all_to_all x1, starting transfers between devices, per_device(): lax.all_to_all(spectra, 'freq', split_axis=2, concat_axis=0, tiled=True)  3.47 us
    dot_general x1, matrix products, per_device(): jnp.einsum('frs,fn->rns', widened[:, 0], cosine_table, precision=lax.Prec...  2.01 us
    dot_general x1, matrix products, column_products(): lax.dot_general(v_local, x_local, (((3,), (1,)), ((), ())), preferred_ele...  1.65 us
    another operation x1, local copies, waits for them, and re-layouts, finish_spectrum(): return jnp.stack([real_part, imag_part], axis=0).astype(jnp.bfloat16)  1.18 us
  transfers between devices with their start and end apart: 4, of which 3 were waited for; matrix products, arithmetic and copies ran while one was open for 0% of the time, Pallas kernels for 0%

profile of v1, /device:TPU:0, one launch (start us, length us, event | category | flops | bytes accessed | tf_op | source)
XLA Modules:
  0.0 50.2 jit_solution(13044085766389996139)
XLA Ops:
  0.0 0.8 %iota_compare_fusion.2 = pred[2,112]{1,0:T(4,128)(4,1)S(1)} fusion(s32[2]{0:T(128)} %bitcast.117), kind=kLoop, calls=%fused_computation.53 | loop fusion | flops 224 | bytes 232 | tf_op jit(solution)/shard_map/lt | solution.py:50
  0.8 0.4 copy-done
  1.2 1.7 %fusion.1 = f32[2,2,112,2,512]{4,2,3,1,0:T(8,128)S(1)} fusion(bf16[1,2,512,512]{3,2,1,0:T(8,128)(2,1)S(1)} %copy-done, bf16[1,1,2,2,112,512]{5,4,3,2,1,0:T(8,128)(2,1)} %param.6), kind=kOutput, calls=%fused_computation.5 | convolution fusion | flops 469762048 | bytes 3342336 | tf_op jit(solution)/shard_map/dot_general | solution.py:44
  2.9 0.2 fusion.13
  3.1 0.0 copy-start.2
  3.2 0.1 broadcast_in_dim.29
  3.3 0.1 constant_dynamic-slice_fusion
  3.4 3.1 %collective-permute-start = (bf16[1,1,2,112,512]{4,3,2,1,0:T(8,128)(2,1)S(1)}, bf16[1,1,2,112,512]{4,3,2,1,0:T(8,128)(2,1)S(1)}, u32[]{:S(2)}, u32[]{:S(2)}) collective-permute-start(bf16[1,1,2,112,512]{4,3,2,1,0:T(8,128)(2,1)S(1)} %get-tuple-element.9), channel_id=1, source_target_pairs={{0,4},{4,8},{8,12},{12,0},{1,5},{5,9},{9,13},{13,1},{2,6},{6,10},{... | collective-permute-start | bytes 688136 | tf_op jit(solution)/shard_map/ppermute | solution.py:30
  6.4 2.1 %collective-permute-start.2 = (bf16[1,1,2,112,512]{4,3,2,1,0:T(8,128)(2,1)S(1)}, bf16[1,1,2,112,512]{4,3,2,1,0:T(8,128)(2,1)S(1)}, u32[]{:S(2)}, u32[]{:S(2)}) collective-permute-start(bf16[1,1,2,112,512]{4,3,2,1,0:T(8,128)(2,1)S(1)} %get-tuple-element.7), channel_id=1, source_target_pairs={{0,12},{4,0},{8,4},{12,8},{1,13},{5,1},{9,5},{13,9},{2,14},{6,2},{... | collective-permute-start | bytes 688136 | tf_op jit(solution)/shard_map/ppermute | solution.py:30
  8.5 0.9 %collective-permute-start.1 = (bf16[1,1,2,112,512]{4,3,2,1,0:T(8,128)(2,1)S(1)}, bf16[1,1,2,112,512]{4,3,2,1,0:T(8,128)(2,1)S(1)}, u32[]{:S(2)}, u32[]{:S(2)}) collective-permute-start(bf16[1,1,2,112,512]{4,3,2,1,0:T(8,128)(2,1)S(1)} %get-tuple-element.8), channel_id=1, source_target_pairs={{0,8},{4,12},{8,0},{12,4},{1,9},{5,13},{9,1},{13,5},{2,10},{6,14},... | collective-permute-start | bytes 688136 | tf_op jit(solution)/shard_map/ppermute | solution.py:30
  9.5 5.5 %collective-permute-done = bf16[1,1,2,112,512]{4,3,2,1,0:T(8,128)(2,1)S(1)} collective-permute-done((bf16[1,1,2,112,512]{4,3,2,1,0:T(8,128)(2,1)S(1)}, bf16[1,1,2,112,512]{4,3,2,1,0:T(8,128)(2,1)S(1)}, u32[]{:S(2)}, u32[]{:S(2)}) %collective-permute-start) | collective-permute-done | bytes 229408 | tf_op jit(solution)/shard_map/ppermute | solution.py:30
  14.9 0.1 broadcast_in_dim.29.clone
  15.0 13.8 %collective-permute-done.1 = bf16[1,1,2,112,512]{4,3,2,1,0:T(8,128)(2,1)S(1)} collective-permute-done((bf16[1,1,2,112,512]{4,3,2,1,0:T(8,128)(2,1)S(1)}, bf16[1,1,2,112,512]{4,3,2,1,0:T(8,128)(2,1)S(1)}, u32[]{:S(2)}, u32[]{:S(2)}) %collective-permute-start.1) | collective-permute-done | bytes 229408 | tf_op jit(solution)/shard_map/ppermute | solution.py:30
  28.9 0.0 copy-start.1
  28.9 0.7 %convolution_bitcast_fusion = f32[2,256,2,512]{1,3,0,2:T(8,128)S(1)} fusion(bf16[4,2,112,512]{3,2,0,1:T(8,128)(2,1)S(1)} %bitcast_dynamic-update-slice_fusion.2, bf16[1,4,2,112,256]{4,3,2,1,0:T(8,128)(2,1)S(1)} %copy-done.2), kind=kOutput, calls=%fused_computation.4 | convolution fusion | flops 469762048 | bytes 3473408 | tf_op jit(solution)/shard_map/dot_general | solution.py:57
  29.6 0.1 fusion.18
  29.7 0.1 fusion.17
  29.8 0.1 pad_maximum_fusion
  29.8 1.2 %copy.36 = bf16[1,2,256,512]{3,1,0,2:T(2,128)(2,1)} copy(bf16[1,2,256,512]{2,3,1,0:T(8,128)(2,1)S(1)} %pad_maximum_fusion) | data formatting | bytes 1048576 | tf_op jit(solution)/shard_map/stack | solution.py:65
  31.0 3.5 %all-to-all-start = ((bf16[1,2,256,512]{3,1,0,2:T(2,128)(2,1)}), bf16[1,2,256,512]{3,1,0,2:T(2,128)(2,1)S(1)}, u32[]{:S(2)}, u32[]{:S(2)}) async-start(bf16[1,2,256,512]{3,1,0,2:T(2,128)(2,1)} %copy.36), calls=%async_computation | async-start | bytes 1048576 | tf_op jit(solution)/shard_map/all_to_all | solution.py:80
  34.5 8.8 %all-to-all-done = bf16[1,2,256,512]{3,1,0,2:T(2,128)(2,1)S(1)} async-done(((bf16[1,2,256,512]{3,1,0,2:T(2,128)(2,1)}), bf16[1,2,256,512]{3,1,0,2:T(2,128)(2,1)S(1)}, u32[]{:S(2)}, u32[]{:S(2)}) %all-to-all-start) | async-done | bytes 524320 | tf_op jit(solution)/shard_map/all_to_all | solution.py:80
  43.3 0.4 copy.55
  43.7 2.0 %fusion.19 = f32[32,64,512]{2,0,1:T(8,128)S(1)} fusion(bf16[4,2,64,512]{3,0,2,1:T(4,128)(2,1)S(1)} %bitcast.113, s32[4]{0:T(128)S(1)} %iota_add_fusion), kind=kOutput, calls=%fused_computation.34 | convolution fusion | flops 50333440 | bytes 4456960 | tf_op jit(solution)/shard_map/frs,fn->rns/dot_general | solution.py:84
  45.7 4.5 %bitcast_select_fusion = f32[64,32,512]{2,1,0:T(8,128)} fusion(f32[32,64,512]{2,0,1:T(8,128)S(1)} %fusion.19, s32[64,512]{1,0:T(8,128)S(1)} %get-tuple-element.11, s32[64,512]{1,0:T(8,128)S(1)} %get-tuple-element.10, bf16[4,2,64,512]{3,0,2,1:T(4,128)(2,1)S(1)} %bitcast.114, s32[4]{0:T(128)S(1)} %iota_add_fusion), kind=kOutput, calls=%fused_computation | convolution fusion | flops 56624896 | bytes 8913408 | tf_op jit(solution)/shard_map/frs,fn->rns/dot_general | solution.py:86
  (11 shorter events, 0.2 us)
Async XLA Ops:
  0.0 1.2 %copy-start = (bf16[1,2,512,512]{3,2,1,0:T(8,128)(2,1)S(1)}, bf16[1,2,512,512]{3,2,1,0:T(8,128)(2,1)}, u32[]{:S(2)}) copy-start(bf16[1,2,512,512]{3,2,1,0:T(8,128)(2,1)} %param.5) | copy-start | bytes 3145732
  3.1 25.8 %copy-start.2 = (bf16[1,4,2,112,256]{4,3,2,1,0:T(8,128)(2,1)S(1)}, bf16[1,4,2,112,256]{4,3,2,1,0:T(8,128)(2,1)}, u32[]{:S(2)}) copy-start(bf16[1,4,2,112,256]{4,3,2,1,0:T(8,128)(2,1)} %param.7) | copy-start | bytes 1376260
  3.4 11.6 %collective-permute-start = (bf16[1,1,2,112,512]{4,3,2,1,0:T(8,128)(2,1)S(1)}, bf16[1,1,2,112,512]{4,3,2,1,0:T(8,128)(2,1)S(1)}, u32[]{:S(2)}, u32[]{:S(2)}) collective-permute-start(bf16[1,1,2,112,512]{4,3,2,1,0:T(8,128)(2,1)S(1)} %get-tuple-element.9), channel_id=1, source_target_pairs={{0,4},{4,8},{8,12},{12,0},{1,5},{5,9},{9,13},{13,1},{2,6},{6,10},{... | collective-permute-start | bytes 688136 | tf_op jit(solution)/shard_map/ppermute | solution.py:30
  6.4 22.4 %collective-permute-start.2 = (bf16[1,1,2,112,512]{4,3,2,1,0:T(8,128)(2,1)S(1)}, bf16[1,1,2,112,512]{4,3,2,1,0:T(8,128)(2,1)S(1)}, u32[]{:S(2)}, u32[]{:S(2)}) collective-permute-start(bf16[1,1,2,112,512]{4,3,2,1,0:T(8,128)(2,1)S(1)} %get-tuple-element.7), channel_id=1, source_target_pairs={{0,12},{4,0},{8,4},{12,8},{1,13},{5,1},{9,5},{13,9},{2,14},{6,2},{... | collective-permute-start | bytes 688136 | tf_op jit(solution)/shard_map/ppermute | solution.py:30
  8.5 20.3 %collective-permute-start.1 = (bf16[1,1,2,112,512]{4,3,2,1,0:T(8,128)(2,1)S(1)}, bf16[1,1,2,112,512]{4,3,2,1,0:T(8,128)(2,1)S(1)}, u32[]{:S(2)}, u32[]{:S(2)}) collective-permute-start(bf16[1,1,2,112,512]{4,3,2,1,0:T(8,128)(2,1)S(1)} %get-tuple-element.8), channel_id=1, source_target_pairs={{0,8},{4,12},{8,0},{12,4},{1,9},{5,13},{9,1},{13,5},{2,10},{6,14},... | collective-permute-start | bytes 688136 | tf_op jit(solution)/shard_map/ppermute | solution.py:30
  28.9 5.6 %copy-start.1 = (s32[2,64,512]{2,1,0:T(8,128)S(1)}, s32[2,64,512]{2,1,0:T(8,128)}, u32[]{:S(2)}) copy-start(s32[2,64,512]{2,1,0:T(8,128)} %param.9) | copy-start | bytes 786436
  31.0 12.3 %all-to-all-start = ((bf16[1,2,256,512]{3,1,0,2:T(2,128)(2,1)}), bf16[1,2,256,512]{3,1,0,2:T(2,128)(2,1)S(1)}, u32[]{:S(2)}, u32[]{:S(2)}) async-start(bf16[1,2,256,512]{3,1,0,2:T(2,128)(2,1)} %copy.36), calls=%async_computation | async-start | bytes 1048576 | tf_op jit(solution)/shard_map/all_to_all | solution.py:80
